TPU v7x, 256 devices: a whole 4x4x8 slice. The times are simulated.
256 devices in a mesh: kv: 2 (over core), pg: 128 (over x, z, y).
Axes of the slice: x: 4, y: 4, z: 8, core: 2. Of those that a mesh axis runs over, the one named last changes fastest.
Arguments:
- layer_hidden_input: bfloat16 [16384, 2560], P('pg'), may hold values from -6 to 6
- norm_scale_vector: float32 [2560], replicated, may hold values from 0.1 to 1.9
- expert_choice_index: int32 [16384, 6], P('pg'), may hold values from 0 to 63, all different within a row; in each aligned block of 128 rows (0 to 127, 128 to 255, ...) at most 16 rows name the same one
- expert_choice_weight: float32 [16384, 6], P('pg'), may hold values from 0.05 to 0.35
- request_of_token: int32 [16384], P('pg'), may hold values from 0 to 255, never falling along the last dimension, each value on 1 to 512 neighbouring positions
- adapter_of_request: int32 [256], replicated, may hold values from 0 to 63
- adapter_of_slot: int32 [128], replicated, may hold values from 0 to 63, as said below
- expert_gate_up_weight: bfloat16 [128, 2560, 2, 768], P('pg', None, None, 'kv'), may hold values from -0.125 to 0.125
- expert_down_weight: bfloat16 [128, 768, 2560], P('pg', 'kv'), may hold values from -0.15625 to 0.15625
- adapter_down_weight: bfloat16 [128, 2560, 8], P('pg'), may hold values from -0.125 to 0.125
- adapter_up_weight: bfloat16 [128, 8, 2560], P('pg', None, 'kv'), may hold values from -0.75 to 0.75
Outputs:
- mixed: bfloat16 [16384, 2560], P('pg', 'kv')
Inputs may be any that keep to these rules, and one draw needn't show every extreme that they name: `expert_choice_index`: each row names 6 different experts. The 128 rows of one index of pg name one expert at most 16 times; some expert is named exactly 16 times by the rows of some index. `adapter_of_slot`: every adapter is held by exactly two slots. `request_of_token`: tokens of one request stand in a row; request numbers never fall along the tokens.
All inputs are finite; a program needn't handle non-finite values.
Results may differ from a plain program's by a relative error of at most 0.013.
Values may be sent and summed in bfloat16 or wider, within the bound.
No kernel may reach another device: no remote copies, remote signals or barrier semaphores. Data moves between devices by JAX's collectives and lax.ppermute only.
A program may use at most 128 MiB of HBM per device.

v0:
```python
import jax
import jax.numpy as jnp
from jax import lax
from jax.sharding import PartitionSpec as P

PG_AXES = ("px", "pz", "py")


def normalize(states, gain_vector):
    values = states.astype(jnp.float32)
    inverse_rms = lax.rsqrt(jnp.mean(values * values, axis=-1, keepdims=True) + 1e-06)
    return (values * inverse_rms * gain_vector).astype(jnp.bfloat16)


def expert_half(expert_rows, expert_gate_up_weight, expert_down_weight):
    gate_up = jnp.einsum(
        "rd,dgf->rgf", expert_rows, expert_gate_up_weight[0], preferred_element_type=jnp.float32
    )
    hidden = (jax.nn.silu(gate_up[:, 0]) * gate_up[:, 1]).astype(jnp.bfloat16)
    local_units = hidden.shape[1]
    piece_count = 2 // lax.axis_size("kv")
    piece_units = local_units // piece_count
    quarter = jnp.dot(
        hidden, expert_down_weight[0, 0:piece_units], preferred_element_type=jnp.float32
    )
    summed = quarter.astype(jnp.bfloat16).astype(jnp.float32)
    return lax.psum_scatter(summed.astype(jnp.bfloat16), "kv", scatter_dimension=1, tiled=True)


def rank_in_expert(flat_ids, expert_count):
    onehot = (flat_ids[:, None] == jnp.arange(expert_count, dtype=jnp.int32)[None, :]).astype(
        jnp.bfloat16
    )
    entries = flat_ids.shape[0]
    lower = (
        jnp.arange(entries, dtype=jnp.int32)[:, None]
        >= jnp.arange(entries, dtype=jnp.int32)[None, :]
    ).astype(jnp.bfloat16)
    running = jnp.dot(lower, onehot, preferred_element_type=jnp.float32)
    return (jnp.sum(running * onehot.astype(jnp.float32), axis=1) - 1.0).astype(jnp.int32)


def place_rows(slot_table, slot_total, normalized_input):
    slot_ids = jnp.arange(slot_total, dtype=jnp.int32)
    hits = jnp.zeros((slot_total, slot_table[0].shape[0]), jnp.float32)
    for table in slot_table:
        hits = hits + jnp.sum(
            (table[None, :, :] == slot_ids[:, None, None]).astype(jnp.float32), axis=2
        )
    placed = jnp.dot(
        hits.astype(jnp.bfloat16), normalized_input, preferred_element_type=jnp.float32
    )
    return placed.astype(jnp.bfloat16)


def collect_rows(slot_table, slot_total, weights, gathered):
    slot_ids = jnp.arange(slot_total, dtype=jnp.int32)
    combine = jnp.zeros((weights.shape[0], slot_total), jnp.float32)
    for table in slot_table:
        combine = combine + jnp.sum(
            jnp.where(table[:, :, None] == slot_ids[None, None, :], weights[:, :, None], 0.0),
            axis=1,
        )
    upper_part = combine.astype(jnp.bfloat16)
    lower_part = (combine - upper_part.astype(jnp.float32)).astype(jnp.bfloat16)
    return jnp.dot(upper_part, gathered, preferred_element_type=jnp.float32) + jnp.dot(
        lower_part, gathered, preferred_element_type=jnp.float32
    )


def on_device(
    layer_hidden_input,
    norm_scale_vector,
    expert_choice_index,
    expert_choice_weight,
    request_of_token,
    adapter_of_request,
    adapter_of_slot,
    expert_gate_up_weight,
    expert_down_weight,
    adapter_down_weight,
    adapter_up_weight,
):
    tok_rows, model_width = layer_hidden_input.shape
    top_count = expert_choice_index.shape[1]
    pg_size = lax.axis_size(PG_AXES)
    expert_count = pg_size // 2
    slot_cap = 4 * tok_rows * top_count // (3 * expert_count)
    half_width = model_width // lax.axis_size("kv")
    kv_index = lax.axis_index("kv")
    normalized_input = normalize(layer_hidden_input, norm_scale_vector)
    own_features = lax.dynamic_slice_in_dim(
        normalized_input, kv_index * half_width, half_width, axis=1
    )
    down_own = lax.dynamic_slice_in_dim(
        adapter_down_weight[0], kv_index * half_width, half_width, axis=0
    )
    rank_half = down_own.shape[1]
    packed = jnp.concatenate([down_own.T, adapter_up_weight[0]], axis=0)
    flat_ids = expert_choice_index.reshape(-1)
    slot_rank = rank_in_expert(flat_ids, expert_count)
    rank_table = slot_rank.reshape(tok_rows, top_count)
    first_slot = 2 * expert_choice_index * slot_cap + rank_table
    second_slot = first_slot + slot_cap
    slot_total = pg_size * slot_cap
    outbox = place_rows((first_slot, second_slot), slot_total, own_features).reshape(
        pg_size, slot_cap, half_width
    )
    inbox_half = lax.all_to_all(outbox, PG_AXES, split_axis=0, concat_axis=0, tiled=True)
    inbox_half, packed = lax.optimization_barrier((inbox_half, packed))
    packed_all = packed
    for axis_name in reversed(PG_AXES):
        packed_all = lax.all_gather(packed_all, axis_name, axis=0, tiled=False)
    packed_all = packed_all.reshape((pg_size,) + packed.shape)
    inbox_rows = lax.all_gather(
        inbox_half.reshape(pg_size * slot_cap, half_width), "kv", axis=1, tiled=True
    )
    half_out = expert_half(inbox_rows, expert_gate_up_weight, expert_down_weight)
    half_out, packed_all = lax.optimization_barrier((half_out, packed_all))
    results = lax.all_to_all(
        half_out.reshape(pg_size, slot_cap, half_width),
        PG_AXES,
        split_axis=0,
        concat_axis=0,
        tiled=True,
    )
    moe_sum = collect_rows(
        (first_slot, second_slot),
        slot_total,
        expert_choice_weight,
        results.reshape(slot_total, half_width),
    )
    request_count = adapter_of_request.shape[0]
    owner_table = request_of_token[:, None] == jnp.arange(request_count, dtype=jnp.int32)[None, :]
    token_adapter = jnp.sum(jnp.where(owner_table, adapter_of_request[None, :], 0), axis=1)
    slot_count = packed_all.shape[0]
    down_all = packed_all[:, 0:rank_half, :].reshape(slot_count * rank_half, half_width)
    up_all = packed_all[:, rank_half:, :].reshape(slot_count * rank_half, half_width)
    partial_rank = lax.dot_general(
        own_features, down_all, (((1,), (1,)), ((), ())), preferred_element_type=jnp.float32
    )
    rank_projected = lax.psum(partial_rank, "kv").reshape(tok_rows, slot_count, rank_half)
    matched = adapter_of_slot[None, :, None] == token_adapter[:, None, None]
    rank_projected = jnp.where(matched, rank_projected, 0.0).astype(jnp.bfloat16)
    flat_low = rank_projected.reshape(tok_rows, slot_count * rank_half)
    adapter_total_output = jnp.dot(flat_low, up_all, preferred_element_type=jnp.float32)
    return (moe_sum + adapter_total_output).astype(jnp.bfloat16)


def solution(mesh):
    kv_count = mesh.shape["kv"]
    pg_count = mesh.shape["pg"]
    y_count = 4 if pg_count % 4 == 0 else 1
    rest = pg_count // y_count
    z_count = 8 if rest % 8 == 0 else rest
    x_count = rest // z_count
    split_mesh = jax.sharding.Mesh(
        mesh.devices.reshape(kv_count, x_count, z_count, y_count), ("kv",) + PG_AXES
    )
    pg = PG_AXES
    placed = (
        P(pg, None),
        P(),
        P(pg, None),
        P(pg, None),
        P(pg),
        P(),
        P(),
        P(pg, None, None, "kv"),
        P(pg, "kv", None),
        P(pg, None, None),
        P(pg, None, "kv"),
    )
    return jax.shard_map(
        on_device, mesh=split_mesh, in_specs=placed, out_specs=P(pg, "kv"), check_vma=False
    )
```

profile of v0, /device:TPU:2, one launch (start us, length us, event | category | flops | bytes accessed | tf_op | source)
XLA Modules:
  0.0 468.3 jit_solution(15037000671731903780)
XLA Ops:
  6.5 0.0 copy-start
  6.5 1.4 convert_element_type.66
  7.9 0.0 copy-start.2
  7.9 1.8 multiply_reduce_fusion
  9.7 0.8 copy.50
  10.5 0.1 eq.98
  10.6 0.4 fusion.22
  11.0 0.1 convert_element_type.61
  11.1 0.1 copy.51
  11.2 0.7 broadcast_add_fusion
  11.9 0.8 dynamic-slice.1
  12.7 1.7 convert_reduce_fusion
  14.4 3.9 convolution_convert_fusion.1
  18.3 0.0 copy-done.2
  18.3 16.1 %all-to-all-start = ((bf16[128,16,1280]{2,1,0:T(8,128)(2,1)}), bf16[128,16,1280]{2,1,0:T(8,128)(2,1)}, u32[]{:S(2)}, u32[]{:S(2)}) async-start(bf16[128,16,1280]{2,1,0:T(8,128)(2,1)} %bitcast.33), calls=%async_computation | async-start | bytes 10485760 | tf_op jit(solution)/shard_map/all_to_all | solution.py:109
  34.4 0.0 all-gather.9.cloned.1.call-start
  34.4 0.0 copy-done.5
  34.5 0.0 copy-done.4
  34.5 119.2 %all-to-all-done = bf16[128,16,1280]{2,1,0:T(8,128)(2,1)} async-done(((bf16[128,16,1280]{2,1,0:T(8,128)(2,1)}), bf16[128,16,1280]{2,1,0:T(8,128)(2,1)}, u32[]{:S(2)}, u32[]{:S(2)}) %all-to-all-start) | async-done | bytes 5242912 | tf_op jit(solution)/shard_map/all_to_all | solution.py:109
  153.7 13.0 %all-gather = bf16[64,1280]{1,0:T(8,128)(2,1)} all-gather(bf16[16,1280]{1,0:T(8,128)(2,1)S(1)} %pad_maximum_fusion), channel_id=2, replica_groups=mesh['kv'=2,'px'=4,'pz'=8,'py'=4] {'py'}, dimensions={0}, use_global_device_ids=true | all-gather | bytes 204800 | tf_op jit(solution)/shard_map/all_gather | solution.py:113
  166.6 0.0 all-gather.9.cloned.1.call-update
  166.6 0.0 all-gather.7.cloned.1.call-start
  166.7 0.7 all-gather.7.cloned.1.call-update
  167.4 0.0 all-gather.11.cloned.1.call-start
  167.4 33.2 %all-gather.9.cloned.1.call-done = bf16[32,16,1280]{2,1,0:T(8,128)(2,1)} async-done(((bf16[4,16,1280]{2,1,0:T(8,128)(2,1)}), bf16[32,16,1280]{2,1,0:T(8,128)(2,1)}) %all-gather.9.cloned.1.call-update) | async-done | bytes 1310736 | tf_op jit(solution)/shard_map/all_gather | solution.py:113
  200.6 0.0 all-gather.11.cloned.1.call-update
  200.6 0.0 reduce-scatter.2.cloned.1.call-start
  200.7 28.5 %all-gather.7.cloned.1.call-done = bf16[2048,2560]{1,0:T(8,128)(2,1)} async-done(((bf16[2048,1280]{1,0:T(8,128)(2,1)}), bf16[2048,2560]{1,0:T(8,128)(2,1)}) %all-gather.7.cloned.1.call-update) | async-done | bytes 10485776 | tf_op jit(solution)/shard_map/all_gather | solution.py:115
  229.1 12.2 %fusion = f32[2048,2,384]{2,0,1:T(8,128)S(1)} fusion(bf16[2048,2560]{1,0:T(8,128)(2,1)} %all-gather.7.cloned.1.call-done, bf16[2560,2,384]{2,1,0:T(2,128)(2,1)} %bitcast.40), kind=kOutput, calls=%fused_computation.1 | convolution fusion | flops 8053063680 | bytes 20709376 | tf_op jit(solution)/shard_map/rd,dgf->rgf/dot_general | solution.py:16
  241.3 0.0 copy-done
  241.3 8.2 %convolution_convert_fusion = bf16[2048,2560]{1,0:T(8,128)(2,1)} fusion(bf16[1,384,2560]{2,1,0:T(8,128)(2,1)S(1)} %copy-done, f32[2048,2,384]{2,0,1:T(8,128)S(1)} %fusion), kind=kOutput, calls=%fused_computation | convolution fusion | flops 4036493312 | bytes 18743296 | tf_op jit(solution)/shard_map/dot_general | solution.py:23
  249.5 0.0 reduce-scatter.2.cloned.1.call-update
  249.5 41.8 %all-gather.11.cloned.1.call-done = bf16[32,4,16,1280]{3,2,1,0:T(8,128)(2,1)} async-done(((bf16[8,4,16,1280]{3,2,1,0:T(8,128)(2,1)}), bf16[32,4,16,1280]{3,2,1,0:T(8,128)(2,1)}) %all-gather.11.cloned.1.call-update) | async-done | bytes 5242896 | tf_op jit(solution)/shard_map/all_gather | solution.py:113
  291.3 27.9 %reduce-scatter.2.cloned.1.call-done = bf16[2048,1280]{1,0:T(8,128)(2,1)} async-done(((bf16[2048,2560]{1,0:T(8,128)(2,1)}), bf16[2048,1280]{1,0:T(8,128)(2,1)}) %reduce-scatter.2.cloned.1.call-update) | async-done | bytes 5242896 | tf_op jit(solution)/shard_map/reduce_scatter | solution.py:27
  319.2 14.4 %all-to-all-start.1 = ((bf16[128,16,1280]{2,1,0:T(8,128)(2,1)}), bf16[128,16,1280]{2,1,0:T(8,128)(2,1)}, u32[]{:S(2)}, u32[]{:S(2)}) async-start(bf16[128,16,1280]{2,1,0:T(8,128)(2,1)} %bitcast.34), calls=%async_computation.2 | async-start | bytes 10485760 | tf_op jit(solution)/shard_map/all_to_all | solution.py:120
  333.7 0.0 copy-done.7
  333.7 0.0 copy-done.9
  333.7 0.2 select_reduce_fusion.2
  333.8 0.0 copy-done.8
  333.9 0.7 broadcast_compare_fusion
  334.6 0.0 copy-done.6
  334.6 3.5 select_reduce_fusion
  338.0 2.9 fusion.18
  340.9 5.3 %all-reduce.1 = bf16[128,128,8]{0,2,1:T(8,128)(2,1)} all-reduce(f32[128,128,8]{0,2,1:T(8,128)S(1)} %fusion.18), channel_id=1, replica_groups=mesh['kv'=2,'px'=4,'pz'=8,'py'=4] {'kv'}, use_global_device_ids=true, to_apply=%region_8.9 | all-reduce | flops 131072 | bytes 786432 | tf_op jit(solution)/shard_map/psum | solution.py:142
  346.2 3.3 fusion.10
  349.5 104.3 %all-to-all-done.1 = bf16[128,16,1280]{2,1,0:T(8,128)(2,1)} async-done(((bf16[128,16,1280]{2,1,0:T(8,128)(2,1)}), bf16[128,16,1280]{2,1,0:T(8,128)(2,1)}, u32[]{:S(2)}, u32[]{:S(2)}) %all-to-all-start.1) | async-done | bytes 5242912 | tf_op jit(solution)/shard_map/all_to_all | solution.py:120
  453.8 3.8 fusion.26
  457.6 4.2 fusion.13
  (14 shorter events, 0.0 us)
Async XLA Ops:
  6.5 234.8 %copy-start = (bf16[1,384,2560]{2,1,0:T(8,128)(2,1)S(1)}, bf16[1,384,2560]{2,1,0:T(8,128)(2,1)}, u32[]{:S(2)}) copy-start(bf16[1,384,2560]{2,1,0:T(8,128)(2,1)} %param.19) | copy-start | bytes 5898244
  7.9 10.4 %copy-start.2 = (f32[128,2560]{1,0:T(8,128)}, f32[128,2560]{1,0:T(8,128)S(1)}, u32[]{:S(2)}) copy-start(f32[128,2560]{1,0:T(8,128)S(1)} %convert_element_type.66) | copy-start | bytes 3932164
  18.3 16.1 %copy-start.5 = (bf16[1,2560,8]{1,2,0:T(8,128)(2,1)S(1)}, bf16[1,2560,8]{1,2,0:T(8,128)(2,1)}, u32[]{:S(2)}) copy-start(bf16[1,2560,8]{1,2,0:T(8,128)(2,1)} %param.20) | copy-start | bytes 122884
  18.3 16.2 %copy-start.4 = (bf16[1,8,1280]{2,1,0:T(8,128)(2,1)S(1)}, bf16[1,8,1280]{2,1,0:T(8,128)(2,1)}, u32[]{:S(2)}) copy-start(bf16[1,8,1280]{2,1,0:T(8,128)(2,1)} %param.21) | copy-start | bytes 61444
  18.3 135.3 %all-to-all-start = ((bf16[128,16,1280]{2,1,0:T(8,128)(2,1)}), bf16[128,16,1280]{2,1,0:T(8,128)(2,1)}, u32[]{:S(2)}, u32[]{:S(2)}) async-start(bf16[128,16,1280]{2,1,0:T(8,128)(2,1)} %bitcast.33), calls=%async_computation | async-start | bytes 10485760 | tf_op jit(solution)/shard_map/all_to_all | solution.py:109
  34.4 166.2 %all-gather.9.cloned.1.call-start = ((), (), s32[]{:S(2)}) async-start(), calls=%async_computation.5 | async-start | bytes 1474560 | tf_op jit(solution)/shard_map/all_gather | solution.py:113
  166.6 62.5 %all-gather.7.cloned.1.call-start = ((), (), s32[]{:S(2)}) async-start(), calls=%async_computation.3 | async-start | bytes 15728640 | tf_op jit(solution)/shard_map/all_gather | solution.py:115
  167.4 123.9 %all-gather.11.cloned.1.call-start = ((), (), s32[]{:S(2)}) async-start(), calls=%async_computation.6 | async-start | bytes 6553600 | tf_op jit(solution)/shard_map/all_gather | solution.py:113
  200.6 118.6 %reduce-scatter.2.cloned.1.call-start = ((), (), s32[]{:S(2)}) async-start(), calls=%async_computation.4 | async-start | bytes 15728640 | tf_op jit(solution)/shard_map/reduce_scatter | solution.py:27
  319.2 14.4 %copy-start.7 = (s32[256]{0:T(256)S(1)}, s32[256]{0:T(256)}, u32[]{:S(2)}) copy-start(s32[256]{0:T(256)} %param.16) | copy-start | bytes 3076
  319.2 14.5 %copy-start.9 = (s32[128]{0:T(128)S(1)}, s32[128]{0:T(128)}, u32[]{:S(2)}) copy-start(s32[128]{0:T(128)} %param.15) | copy-start | bytes 1540
  319.2 14.6 %copy-start.8 = (s32[128]{0:T(128)S(1)}, s32[128]{0:T(128)}, u32[]{:S(2)}) copy-start(s32[128]{0:T(128)} %param.17) | copy-start | bytes 1540
  319.2 15.3 %copy-start.6 = (f32[128,6]{0,1:T(8,128)S(1)}, f32[128,6]{0,1:T(8,128)}, u32[]{:S(2)}) copy-start(f32[128,6]{0,1:T(8,128)} %param.14) | copy-start | bytes 9220
  319.2 134.5 %all-to-all-start.1 = ((bf16[128,16,1280]{2,1,0:T(8,128)(2,1)}), bf16[128,16,1280]{2,1,0:T(8,128)(2,1)}, u32[]{:S(2)}, u32[]{:S(2)}) async-start(bf16[128,16,1280]{2,1,0:T(8,128)(2,1)} %bitcast.34), calls=%async_computation.2 | async-start | bytes 10485760 | tf_op jit(solution)/shard_map/all_to_all | solution.py:120
  453.8 3.8 copy-start.1
  453.8 3.8 copy-start.3
Sparse Core Ops, SparseCore 0:
  166.8 33.7 all-gather.8
  202.4 26.7 all-gather.6
  231.0 60.3 all-gather.10
  293.7 25.4 reduce-scatter.1
where the time goes:
time: 469 us; the launch traced here: 468 us
  waiting for transfers between devices  356 us (76%)
  matrix products  38.7 us (8%)
  starting transfers between devices  30.6 us (7%)
  blocking collectives  18.3 us (4%)
  between operations  13.3 us (3%)
  other arithmetic  9.88 us (2%)
    all_to_all x1, waiting for transfers between devices, on_device(): lax.all_to_all(outbox, PG_AXES, split_axis=0, concat_axis=0, tiled=True)  119 us
    all_to_all x1, waiting for transfers between devices, on_device(): lax.all_to_all(half_out.reshape(pg_size, slot_cap, half_width), PG_AXES,...  104 us
    all_gather x2, waiting for transfers between devices, on_device(): packed_all = lax.all_gather(packed_all, axis_name, axis=0, tiled=False)  75 us
    all_gather x1, waiting for transfers between devices, on_device(): lax.all_gather(inbox_half.reshape(pg_size * slot_cap, half_width), 'kv',...  28.5 us
    reduce_scatter x1, waiting for transfers between devices, expert_half(): lax.psum_scatter(summed.astype(jnp.bfloat16), 'kv', scatter_dimension=1,...  27.9 us
    all_to_all x1, starting transfers between devices, on_device(): lax.all_to_all(outbox, PG_AXES, split_axis=0, concat_axis=0, tiled=True)  16.1 us
    all_to_all x1, starting transfers between devices, on_device(): lax.all_to_all(half_out.reshape(pg_size, slot_cap, half_width), PG_AXES,...  14.4 us
    all_gather x1, blocking collectives, on_device(): packed_all = lax.all_gather(packed_all, axis_name, axis=0, tiled=False)  13 us
  transfers between devices with their start and end apart: 6, of which 6 were waited for; matrix products, arithmetic and copies ran while one was open for 7% of the time, Pallas kernels for 0%

commit v1 on v0

--- a/solution.py
+++ b/solution.py
@@ -4,6 +4,11 @@
 from jax.sharding import PartitionSpec as P
 
 PG_AXES = ("px", "pz", "py")
+
+
+def exchange_gather(block, name, along):
+    sent = jnp.stack([block] * lax.axis_size(name))
+    return jnp.concatenate(lax.all_to_all(sent, name, 0, 0), axis=along)
 
 
 def normalize(states, gain_vector):
@@ -112,9 +117,7 @@
     for axis_name in reversed(PG_AXES):
         packed_all = lax.all_gather(packed_all, axis_name, axis=0, tiled=False)
     packed_all = packed_all.reshape((pg_size,) + packed.shape)
-    inbox_rows = lax.all_gather(
-        inbox_half.reshape(pg_size * slot_cap, half_width), "kv", axis=1, tiled=True
-    )
+    inbox_rows = exchange_gather(inbox_half.reshape(pg_size * slot_cap, half_width), "kv", 1)
     half_out = expert_half(inbox_rows, expert_gate_up_weight, expert_down_weight)
     half_out, packed_all = lax.optimization_barrier((half_out, packed_all))
     results = lax.all_to_all(

time: 469 us -> 517 us (1.10)
  local copies, waits for them, and re-layouts: 1.95 us -> 99.2 us
  waiting for transfers between devices: 356 us -> 280 us
  blocking collectives: 18.3 us -> 32.8 us
  other arithmetic: 9.88 us -> 19 us
    reshape x0 -> x2, local copies, waits for them, and re-layouts: none -> 97.2 us  [exchange_gather(): return jnp.concatenate(lax.all_to_all(sent, name, 0, 0), axis=along)]
    all_gather x2, waiting for transfers between devices: 75 us -> 33.9 us  [on_device(): packed_all = lax.all_gather(packed_all, axis_name, axis=0, tiled=False)]
    all_gather x1 -> x0, waiting for transfers between devices: 28.5 us -> none  [on_device(): lax.all_gather(inbox_half.reshape(pg_size * slot_cap, half_width), 'kv',...]
    all_to_all x0 -> x1, blocking collectives: none -> 14.5 us  [exchange_gather(): return jnp.concatenate(lax.all_to_all(sent, name, 0, 0), axis=along)]
    another operation x0 -> x1, other arithmetic: none -> 9.07 us  [exchange_gather(): sent = jnp.stack([block] * lax.axis_size(name))]
    reduce_scatter x1, waiting for transfers between devices: 27.9 us -> 22.7 us  [expert_half(): lax.psum_scatter(summed.astype(jnp.bfloat16), 'kv', scatter_dimension=1,...]
  transfers between devices with their start and end apart: 6 -> 5, of which waited for: 6 -> 4; matrix products, arithmetic and copies ran while one was open for 7% -> 27% of each run, Pallas kernels for 0% -> 0%
where the time goes in v1:
time: 517 us; the launch traced here: 516 us
  waiting for transfers between devices  280 us (54%)
  local copies, waits for them, and re-layouts  99.2 us (19%)
  matrix products  38.8 us (8%)
  blocking collectives  32.8 us (6%)
  starting transfers between devices  30.6 us (6%)
  other arithmetic  19 us (4%)
  between operations  15 us (3%)
    all_to_all x1, waiting for transfers between devices, on_device(): lax.all_to_all(outbox, PG_AXES, split_axis=0, concat_axis=0, tiled=True)  119 us
    all_to_all x1, waiting for transfers between devices, on_device(): lax.all_to_all(half_out.reshape(pg_size, slot_cap, half_width), PG_AXES,...  104 us
    reshape x2, local copies, waits for them, and re-layouts, exchange_gather(): return jnp.concatenate(lax.all_to_all(sent, name, 0, 0), axis=along)  97.2 us
    all_gather x2, waiting for transfers between devices, on_device(): packed_all = lax.all_gather(packed_all, axis_name, axis=0, tiled=False)  33.9 us
    reduce_scatter x1, waiting for transfers between devices, expert_half(): lax.psum_scatter(summed.astype(jnp.bfloat16), 'kv', scatter_dimension=1,...  22.7 us
    all_to_all x1, starting transfers between devices, on_device(): lax.all_to_all(outbox, PG_AXES, split_axis=0, concat_axis=0, tiled=True)  16.1 us
    all_to_all x1, blocking collectives, exchange_gather(): return jnp.concatenate(lax.all_to_all(sent, name, 0, 0), axis=along)  14.5 us
    all_to_all x1, starting transfers between devices, on_device(): lax.all_to_all(half_out.reshape(pg_size, slot_cap, half_width), PG_AXES,...  14.4 us
  transfers between devices with their start and end apart: 5, of which 4 were waited for; matrix products, arithmetic and copies ran while one was open for 27% of the time, Pallas kernels for 0%

profile of v1, /device:TPU:2, one launch (start us, length us, event | category | flops | bytes accessed | tf_op | source)
XLA Modules:
  0.0 515.6 jit_solution(15852066076589916879)
XLA Ops:
  7.4 0.0 copy-start
  7.4 1.4 convert_element_type.66
  8.7 0.0 copy-start.2
  8.7 1.8 multiply_reduce_fusion
  10.5 0.8 copy.57
  11.3 0.1 eq.98
  11.4 0.4 fusion.21
  11.8 0.1 convert_element_type.61
  12.0 0.1 copy.58
  12.0 0.7 broadcast_add_fusion
  12.8 0.8 dynamic-slice.1
  13.5 1.7 convert_reduce_fusion
  15.2 3.9 convolution_convert_fusion.1
  19.1 0.0 copy-done.2
  19.2 16.1 %all-to-all-start = ((bf16[128,16,1280]{2,1,0:T(8,128)(2,1)}), bf16[128,16,1280]{2,1,0:T(8,128)(2,1)}, u32[]{:S(2)}, u32[]{:S(2)}) async-start(bf16[128,16,1280]{2,1,0:T(8,128)(2,1)} %bitcast.32), calls=%async_computation | async-start | bytes 10485760 | tf_op jit(solution)/shard_map/all_to_all | solution.py:114
  35.2 0.0 all-gather.6.cloned.1.call-start
  35.3 0.0 copy-done.5
  35.3 0.0 copy-done.4
  35.3 119.2 %all-to-all-done = bf16[128,16,1280]{2,1,0:T(8,128)(2,1)} async-done(((bf16[128,16,1280]{2,1,0:T(8,128)(2,1)}), bf16[128,16,1280]{2,1,0:T(8,128)(2,1)}, u32[]{:S(2)}, u32[]{:S(2)}) %all-to-all-start) | async-done | bytes 5242912 | tf_op jit(solution)/shard_map/all_to_all | solution.py:114
  154.5 13.0 %all-gather = bf16[64,1280]{1,0:T(8,128)(2,1)} all-gather(bf16[16,1280]{1,0:T(8,128)(2,1)S(1)} %pad_maximum_fusion.1), channel_id=2, replica_groups=mesh['kv'=2,'px'=4,'pz'=8,'py'=4] {'py'}, dimensions={0}, use_global_device_ids=true | all-gather | bytes 204800 | tf_op jit(solution)/shard_map/all_gather | solution.py:118
  167.5 0.0 all-gather.6.cloned.1.call-update
  167.5 0.0 all-gather.8.cloned.1.call-start
  167.5 33.9 %all-gather.6.cloned.1.call-done = bf16[32,16,1280]{2,1,0:T(8,128)(2,1)} async-done(((bf16[4,16,1280]{2,1,0:T(8,128)(2,1)}), bf16[32,16,1280]{2,1,0:T(8,128)(2,1)}) %all-gather.6.cloned.1.call-update) | async-done | bytes 1310736 | tf_op jit(solution)/shard_map/all_gather | solution.py:118
  201.4 0.0 all-gather.8.cloned.1.call-update
  201.5 0.0 reduce-scatter.2.cloned.1.call-start
  201.5 9.1 %pad_maximum_fusion = bf16[2,2048,1280]{2,1,0:T(8,128)(2,1)} fusion(bf16[1,2048,1280]{2,1,0:T(8,128)(2,1)} %bitcast.4), kind=kLoop, calls=%fused_computation.1 | loop fusion | flops 5242880 | bytes 15728640 | tf_op jit(solution)/shard_map/stack | solution.py:10
  210.6 14.5 %all_to_all.15 = bf16[2,2048,1280]{2,1,0:T(8,128)(2,1)S(1)} all-to-all(bf16[2,2048,1280]{2,1,0:T(8,128)(2,1)} %pad_maximum_fusion), channel_id=1, replica_groups=mesh['kv'=2,'px'=4,'pz'=8,'py'=4] {'kv'}, dimensions={0} | all-to-all | bytes 20971520 | tf_op jit(solution)/shard_map/all_to_all | solution.py:11
  225.1 74.0 %copy.59 = bf16[2048,2,1280]{2,1,0:T(2,128)(2,1)} copy(bf16[2048,2,1280]{2,0,1:T(8,128)(2,1)S(1)} %bitcast.33) | data formatting | bytes 20971520 | tf_op jit(solution)/shard_map/reshape | solution.py:11
  299.0 23.2 %reshape.94 = bf16[2048,2560,1]{1,0,2:T(8,128)(2,1)} reshape(bf16[2048,2,1280]{2,1,0:T(2,128)(2,1)} %copy.59) | data formatting | bytes 20971520 | tf_op jit(solution)/shard_map/reshape | solution.py:11
  322.3 12.2 %fusion = f32[2048,2,384]{2,0,1:T(8,128)S(1)} fusion(bf16[2048,2560,1]{1,0,2:T(8,128)(2,1)} %reshape.94, bf16[2560,2,384]{2,1,0:T(2,128)(2,1)} %bitcast.40), kind=kOutput, calls=%fused_computation.11 | convolution fusion | flops 8053063680 | bytes 20709376 | tf_op jit(solution)/shard_map/rd,dgf->rgf/dot_general | solution.py:21
  334.4 0.0 copy-done
  334.4 8.2 %convolution_convert_fusion = bf16[2048,2560]{1,0:T(8,128)(2,1)} fusion(bf16[1,384,2560]{2,1,0:T(8,128)(2,1)S(1)} %copy-done, f32[2048,2,384]{2,0,1:T(8,128)S(1)} %fusion), kind=kOutput, calls=%fused_computation | convolution fusion | flops 4036493312 | bytes 18743296 | tf_op jit(solution)/shard_map/dot_general | solution.py:28
  342.6 0.0 reduce-scatter.2.cloned.1.call-update
  342.7 0.0 all-gather.8.cloned.1.call-done
  342.7 22.7 %reduce-scatter.2.cloned.1.call-done = bf16[2048,1280]{1,0:T(8,128)(2,1)} async-done(((bf16[2048,2560]{1,0:T(8,128)(2,1)}), bf16[2048,1280]{1,0:T(8,128)(2,1)}) %reduce-scatter.2.cloned.1.call-update) | async-done | bytes 5242896 | tf_op jit(solution)/shard_map/reduce_scatter | solution.py:32
  365.4 14.4 %all-to-all-start.2 = ((bf16[128,16,1280]{2,1,0:T(8,128)(2,1)}), bf16[128,16,1280]{2,1,0:T(8,128)(2,1)}, u32[]{:S(2)}, u32[]{:S(2)}) async-start(bf16[128,16,1280]{2,1,0:T(8,128)(2,1)} %bitcast.34), calls=%async_computation.3 | async-start | bytes 10485760 | tf_op jit(solution)/shard_map/all_to_all | solution.py:123
  379.8 0.0 copy-done.7
  379.8 0.0 copy-done.9
  379.8 0.2 select_reduce_fusion.2
  380.0 0.0 copy-done.8
  380.0 0.7 broadcast_compare_fusion
  380.7 3.5 select_reduce_fusion
  384.2 2.9 fusion.17
  387.0 5.3 %all-reduce.1 = bf16[128,128,8]{0,2,1:T(8,128)(2,1)} all-reduce(f32[128,128,8]{0,2,1:T(8,128)S(1)} %fusion.17), channel_id=1, replica_groups=mesh['kv'=2,'px'=4,'pz'=8,'py'=4] {'kv'}, use_global_device_ids=true, to_apply=%region_8.9 | all-reduce | flops 131072 | bytes 786432 | tf_op jit(solution)/shard_map/psum | solution.py:145
  392.3 3.3 fusion.9
  395.6 104.5 %all-to-all-done.2 = bf16[128,16,1280]{2,1,0:T(8,128)(2,1)} async-done(((bf16[128,16,1280]{2,1,0:T(8,128)(2,1)}), bf16[128,16,1280]{2,1,0:T(8,128)(2,1)}, u32[]{:S(2)}, u32[]{:S(2)}) %all-to-all-start.2) | async-done | bytes 5242912 | tf_op jit(solution)/shard_map/all_to_all | solution.py:123
  500.1 3.8 fusion.25
  503.9 4.2 fusion.12
  (15 shorter events, 0.0 us)
Async XLA Ops:
  7.4 327.1 %copy-start = (bf16[1,384,2560]{2,1,0:T(8,128)(2,1)S(1)}, bf16[1,384,2560]{2,1,0:T(8,128)(2,1)}, u32[]{:S(2)}) copy-start(bf16[1,384,2560]{2,1,0:T(8,128)(2,1)} %param.19) | copy-start | bytes 5898244
  8.7 10.4 %copy-start.2 = (f32[128,2560]{1,0:T(8,128)}, f32[128,2560]{1,0:T(8,128)S(1)}, u32[]{:S(2)}) copy-start(f32[128,2560]{1,0:T(8,128)S(1)} %convert_element_type.66) | copy-start | bytes 3932164
  19.2 16.1 %copy-start.5 = (bf16[1,2560,8]{1,2,0:T(8,128)(2,1)S(1)}, bf16[1,2560,8]{1,2,0:T(8,128)(2,1)}, u32[]{:S(2)}) copy-start(bf16[1,2560,8]{1,2,0:T(8,128)(2,1)} %param.20) | copy-start | bytes 122884
  19.2 16.2 %copy-start.4 = (bf16[1,8,1280]{2,1,0:T(8,128)(2,1)S(1)}, bf16[1,8,1280]{2,1,0:T(8,128)(2,1)}, u32[]{:S(2)}) copy-start(bf16[1,8,1280]{2,1,0:T(8,128)(2,1)} %param.21) | copy-start | bytes 61444
  19.2 135.3 %all-to-all-start = ((bf16[128,16,1280]{2,1,0:T(8,128)(2,1)}), bf16[128,16,1280]{2,1,0:T(8,128)(2,1)}, u32[]{:S(2)}, u32[]{:S(2)}) async-start(bf16[128,16,1280]{2,1,0:T(8,128)(2,1)} %bitcast.32), calls=%async_computation | async-start | bytes 10485760 | tf_op jit(solution)/shard_map/all_to_all | solution.py:114
  35.2 166.2 %all-gather.6.cloned.1.call-start = ((), (), s32[]{:S(2)}) async-start(), calls=%async_computation.5 | async-start | bytes 1474560 | tf_op jit(solution)/shard_map/all_gather | solution.py:118
  167.5 175.2 %all-gather.8.cloned.1.call-start = ((), (), s32[]{:S(2)}) async-start(), calls=%async_computation.6 | async-start | bytes 6553600 | tf_op jit(solution)/shard_map/all_gather | solution.py:118
  201.5 163.9 %reduce-scatter.2.cloned.1.call-start = ((), (), s32[]{:S(2)}) async-start(), calls=%async_computation.4 | async-start | bytes 15728640 | tf_op jit(solution)/shard_map/reduce_scatter | solution.py:32
  365.4 14.4 %copy-start.7 = (s32[256]{0:T(256)S(1)}, s32[256]{0:T(256)}, u32[]{:S(2)}) copy-start(s32[256]{0:T(256)} %param.16) | copy-start | bytes 3076
  365.4 14.4 %copy-start.9 = (s32[128]{0:T(128)S(1)}, s32[128]{0:T(128)}, u32[]{:S(2)}) copy-start(s32[128]{0:T(128)} %param.15) | copy-start | bytes 1540
  365.4 14.6 %copy-start.8 = (s32[128]{0:T(128)S(1)}, s32[128]{0:T(128)}, u32[]{:S(2)}) copy-start(s32[128]{0:T(128)} %param.17) | copy-start | bytes 1540
  365.4 15.3 %copy-start.6 = (f32[128,6]{0,1:T(8,128)S(1)}, f32[128,6]{0,1:T(8,128)}, u32[]{:S(2)}) copy-start(f32[128,6]{0,1:T(8,128)} %param.14) | copy-start | bytes 9220
  365.4 134.7 %all-to-all-start.2 = ((bf16[128,16,1280]{2,1,0:T(8,128)(2,1)}), bf16[128,16,1280]{2,1,0:T(8,128)(2,1)}, u32[]{:S(2)}, u32[]{:S(2)}) async-start(bf16[128,16,1280]{2,1,0:T(8,128)(2,1)} %bitcast.34), calls=%async_computation.3 | async-start | bytes 10485760 | tf_op jit(solution)/shard_map/all_to_all | solution.py:123
  500.1 3.8 copy-start.1
  500.1 3.8 copy-start.3
Sparse Core Ops, SparseCore 0:
  167.6 33.7 all-gather.5
  203.2 57.5 all-gather.7
Sparse Core Ops, SparseCore 1:
  342.7 22.6 reduce-scatter.1
